TPU v7x, 256 devices: a whole 4x4x8 slice. The times are simulated.
256 devices in a mesh: segment: 2 (over core), ctx: 64 (over x, z, y_hi), tp: 2 (over y_lo).
Axes of the slice: x: 4, y: 4 (y_hi: 2, y_lo: 2; y = y_hi * 2 + y_lo), z: 8, core: 2. Of those that a mesh axis runs over, the one named last changes fastest.
Arguments:
- queries: bfloat16 [8192, 32, 128], P('ctx', 'tp'), may hold values from -14 to 14
- keys: bfloat16 [8192, 8, 128], P('ctx', 'tp'), may hold values from -10 to 10
- values: bfloat16 [8192, 8, 128], P('ctx', 'tp'), may hold values from -6 to 6
- layer_in: bfloat16 [8192, 4096], P('ctx', 'tp'), may hold values from -6 to 6
- w_bc: bfloat16 [1, 4096, 1024], P(None, 'tp'), may hold values from -0.09375 to 0.09375
- w_dt: bfloat16 [1, 4096, 64], P(None, 'tp'), may hold values from -0.09375 to 0.09375
- dt_bias: float32 [1, 64], P(None, 'tp'), may hold values from -1 to 1
- decay_rate: float32 [1, 64], P(None, 'tp'), may hold values from 1.2207031e-05 to 0.06
- skip_gain: float32 [1, 64], P(None, 'tp'), may hold values from 0.5 to 2
- out_gain: float32 [1, 64, 64], P(None, 'tp'), may hold values from 0.5 to 1.5
Outputs:
- section_out: bfloat16 [2, 8192, 4096], P('segment', 'ctx', 'tp')
All inputs are finite; a program needn't handle non-finite values.
Results may differ from a plain program's by a relative error of at most 0.002.
Values may be sent and summed in bfloat16 or wider, within the bound.
No kernel may reach another device: no remote copies, remote signals or barrier semaphores. Data moves between devices by JAX's collectives and lax.ppermute only.
A program may use at most 256 MiB of HBM per device.

v0:
```python
import math
import jax
import jax.numpy as jnp
from jax import lax
from jax.sharding import PartitionSpec as P

GROUPS = 4
STATE = 128
EPSILON = 1e-05


def shifted_up(value, axis, distance):
    size = lax.axis_size(axis)
    pairs = [(source, source + distance) for source in range(size - distance)]
    return lax.ppermute(value, axis, pairs)


def swapped(value, axis):
    return lax.ppermute(value, axis, [(0, 1), (1, 0)])


def span_terms(normed, b_rows, c_rows, step_sizes, rate_row, skip_row):
    count_rows, head_count, head_width = normed.shape
    group_count = b_rows.shape[1]
    per_group = head_count // group_count
    state_root = math.sqrt(b_rows.shape[2])
    log_decay = jnp.cumsum(-step_sizes * rate_row[None, :], axis=0)
    lower_mask = jnp.arange(count_rows)[:, None] >= jnp.arange(count_rows)[None, :]
    intersection = (
        jnp.einsum("tgn,sgn->gts", c_rows, b_rows, precision=lax.Precision.HIGHEST) / state_root
    )
    log_gaps = log_decay.T[:, :, None] - log_decay.T[:, None, :]
    decays = jnp.where(lower_mask[None], jnp.exp(jnp.where(lower_mask[None], log_gaps, 0.0)), 0.0)
    mixing = (
        decays.reshape(group_count, per_group, count_rows, count_rows)
        * intersection[:, None]
        * step_sizes.T.reshape(group_count, per_group, 1, count_rows)
    )
    grouped = normed.reshape(count_rows, group_count, per_group, head_width)
    local_part = jnp.einsum(
        "gkts,sgkp->tgkp", mixing, grouped, precision=lax.Precision.HIGHEST
    ).reshape(count_rows, head_count, head_width)
    tail_weight = jnp.exp(log_decay[-1][None, :] - log_decay) * step_sizes
    weighted = (normed * tail_weight[:, :, None]).reshape(
        count_rows, group_count, per_group, head_width
    )
    ending = jnp.einsum(
        "sgkp,sgn->gkpn", weighted, b_rows, precision=lax.Precision.HIGHEST
    ).reshape(head_count, head_width, b_rows.shape[2])
    return (
        log_decay,
        local_part + skip_row[None, :, None] * normed,
        ending,
        jnp.exp(log_decay[-1]),
    )


def span_inflow(log_decay, c_rows, state_in):
    count_rows, group_count, state_n = c_rows.shape
    head_count, head_width = (state_in.shape[0], state_in.shape[1])
    per_group = head_count // group_count
    state_root = math.sqrt(state_n)
    inflow = jnp.einsum(
        "tgn,gkpn->tgkp",
        c_rows,
        state_in.reshape(group_count, per_group, head_width, state_n),
        precision=lax.Precision.HIGHEST,
    )
    return (
        jnp.exp(log_decay)[:, :, None]
        * inflow.reshape(count_rows, head_count, head_width)
        / state_root
    )


def merge_states(earlier, later):
    return (earlier[0] * later[0], later[0][:, None, None] * earlier[1] + later[1])


def exclusive_scan(decay, state, axis):
    place = lax.axis_index(axis)
    size = lax.axis_size(axis)
    incl = (decay, state)
    excl = (jnp.ones_like(decay), jnp.zeros_like(state))
    distance = 1
    while distance < size:
        got = jax.tree.map(lambda a: shifted_up(a, axis, distance), incl)
        present = place >= distance
        got = (jnp.where(present, got[0], 1.0), jnp.where(present, got[1], 0.0))
        excl = merge_states(got, excl)
        if distance * 2 < size:
            incl = merge_states(got, incl)
        distance *= 2
    return excl


def attention_half(queries, keys, values, first_row):
    row_count, q_heads, head_width = queries.shape
    kv_heads = keys.shape[1]
    group_size = q_heads // kv_heads
    score_scale = 1.0 / math.sqrt(head_width)
    last_row = first_row + row_count - 1
    query_place = first_row + jnp.arange(row_count, dtype=jnp.int32)
    grouped = queries.reshape(row_count, kv_heads, group_size, head_width).transpose(1, 2, 0, 3)
    both = jnp.concatenate([keys, values], axis=1)
    both_all = lax.all_gather(both, "ctx", axis=0, tiled=True)
    key_count = both_all.shape[0]
    block_size = math.gcd(key_count, 1024)

    def add_block(block_index, carried):
        row_top, row_total, row_sum = carried
        block_start = block_index * block_size
        block = lax.dynamic_slice_in_dim(both_all, block_start, block_size, 0)
        key_block = block[:, :kv_heads]
        value_block = block[:, kv_heads:]
        scores = (
            jnp.einsum("kgqd,skd->kgqs", grouped, key_block, preferred_element_type=jnp.float32)
            * score_scale
        )
        key_place = block_start + jnp.arange(block_size, dtype=jnp.int32)
        allowed = (query_place[:, None] >= key_place[None, :])[None, None]
        masked = jnp.where(allowed, scores, -1e30)
        new_top = jnp.maximum(row_top, jnp.max(masked, axis=3))
        raw_weight = jnp.where(allowed, jnp.exp(masked - new_top[..., None]), 0.0)
        factor = jnp.exp(row_top - new_top)
        new_total = row_total * factor + jnp.sum(raw_weight, axis=3)
        block_sum = jnp.einsum(
            "kgqs,skd->kgqd",
            raw_weight.astype(jnp.bfloat16),
            value_block,
            preferred_element_type=jnp.float32,
        )
        return (new_top, new_total, row_sum * factor[..., None] + block_sum)

    initial = (
        jnp.full((kv_heads, group_size, row_count), -1e30, jnp.float32),
        jnp.zeros((kv_heads, group_size, row_count), jnp.float32),
        jnp.zeros((kv_heads, group_size, row_count, head_width), jnp.float32),
    )
    block_count = last_row // block_size + 1
    row_top, row_total, row_sum = lax.fori_loop(0, block_count, add_block, initial)
    mixed_out = row_sum / row_total[..., None]
    return (
        mixed_out.transpose(2, 0, 1, 3)
        .reshape(row_count, q_heads * head_width)
        .astype(jnp.bfloat16)
    )


def body(queries, keys, values, layer_in, w_bc, w_dt, dt_bias, decay_rate, skip_gain, out_gain):
    seg = lax.axis_index("segment")
    seg_count = lax.axis_size("segment")
    tp = lax.axis_index("tp")
    tp_count = lax.axis_size("tp")
    row_count, q_heads, head_width = queries.shape
    kv_heads = keys.shape[1]
    first_row = lax.axis_index("ctx") * row_count
    q_share = q_heads // seg_count
    kv_share = kv_heads // seg_count
    q_part = lax.dynamic_slice_in_dim(queries, seg * q_share, q_share, 1)
    k_part = lax.dynamic_slice_in_dim(keys, seg * kv_share, kv_share, 1)
    v_part = lax.dynamic_slice_in_dim(values, seg * kv_share, kv_share, 1)
    attended = attention_half(q_part, k_part, v_part, first_row)
    current = layer_in
    channel_count = current.shape[1]
    heads_dev = dt_bias.shape[1]
    state_width = channel_count // heads_dev
    groups_dev = GROUPS // tp_count
    groups_core = groups_dev // seg_count
    heads_core = heads_dev // seg_count
    half_cols = GROUPS * STATE
    wide_rows = current.astype(jnp.float32)
    part_bc = jnp.dot(current, w_bc[0], preferred_element_type=jnp.float32)
    part_dt = jnp.dot(current, w_dt[0], preferred_element_type=jnp.float32)
    part_sq = jnp.sum(wide_rows * wide_rows, axis=1)

    def columns_for(tp_index):
        group_start = (tp_index * groups_dev + seg * groups_core) * STATE
        head_start = tp_index * heads_dev + seg * heads_core
        return jnp.concatenate(
            [
                lax.dynamic_slice_in_dim(part_bc, group_start, groups_core * STATE, 1),
                lax.dynamic_slice_in_dim(part_bc, half_cols + group_start, groups_core * STATE, 1),
                lax.dynamic_slice_in_dim(part_dt, head_start, heads_core, 1),
                part_sq[:, None],
            ],
            axis=1,
        )

    mine = columns_for(tp)
    theirs = columns_for(tp_count - 1 - tp)
    total = mine + swapped(theirs, "tp")
    width_bc = groups_core * STATE
    sum_b = total[:, :width_bc]
    sum_c = total[:, width_bc : 2 * width_bc]
    sum_dt = total[:, 2 * width_bc : 2 * width_bc + heads_core]
    sum_sq = total[:, 2 * width_bc + heads_core]
    inv_rms = lax.rsqrt(sum_sq / (channel_count * tp_count) + EPSILON)
    own_rows = lax.dynamic_slice_in_dim(
        wide_rows, seg * heads_core * state_width, heads_core * state_width, 1
    )
    normed = (own_rows * inv_rms[:, None]).reshape(row_count, heads_core, state_width)
    b_rows = (sum_b * inv_rms[:, None]).reshape(row_count, groups_core, STATE)
    c_rows = (sum_c * inv_rms[:, None]).reshape(row_count, groups_core, STATE)
    bias = lax.dynamic_slice_in_dim(dt_bias[0], seg * heads_core, heads_core, 0)
    rate = lax.dynamic_slice_in_dim(decay_rate[0], seg * heads_core, heads_core, 0)
    skip = lax.dynamic_slice_in_dim(skip_gain[0], seg * heads_core, heads_core, 0)
    gain = lax.dynamic_slice_in_dim(out_gain[0], seg * heads_core, heads_core, 0)
    step_sizes = jax.nn.softplus(sum_dt * inv_rms[:, None] + bias[None, :])
    log_decay, local_part, ending, span_decay = span_terms(
        normed, b_rows, c_rows, step_sizes, rate, skip
    )
    _, state_in = exclusive_scan(span_decay, ending, "ctx")
    mixed_out = local_part + span_inflow(log_decay, c_rows, state_in)
    power = jnp.mean(mixed_out * mixed_out, axis=2, keepdims=True)
    result = own_rows.reshape(row_count, heads_core, state_width) + gain[
        None
    ] * mixed_out * lax.rsqrt(power + EPSILON)
    state_part = result.reshape(row_count, heads_core * state_width).astype(jnp.bfloat16)
    keep_state = seg == 0
    outgoing = jnp.where(keep_state, attended, state_part)
    incoming = swapped(outgoing, "segment")
    first = jnp.where(keep_state, state_part, incoming)
    second = jnp.where(keep_state, incoming, attended)
    return jnp.concatenate([first, second], axis=1)[None]


def solution(mesh):
    in_specs = (
        P("ctx", "tp", None),
        P("ctx", "tp", None),
        P("ctx", "tp", None),
        P("ctx", "tp"),
        P(None, "tp", None),
        P(None, "tp", None),
        P(None, "tp"),
        P(None, "tp"),
        P(None, "tp"),
        P(None, "tp", None),
    )
    out_specs = P("segment", "ctx", "tp")
    return jax.shard_map(body, mesh=mesh, in_specs=in_specs, out_specs=out_specs, check_vma=False)
```

profile of v0, /device:TPU:239, one launch (start us, length us, event | category | flops | bytes accessed | tf_op | source)
XLA Modules:
  0.0 272.6 jit_solution(10316998573162825746)
XLA Ops:
  6.5 1.2 constant_dynamic-slice_fusion.1
  8.4 1.3 copy.46
  9.8 1.4 fusion.59
  11.2 4.1 %fusion.17 = f32[128,1024]{0,1:T(8,128)S(1)} fusion(bf16[128,2048]{1,0:T(8,128)(2,1)} %param.15, bf16[1,2048,1024]{2,1,0:T(8,128)(2,1)} %param.16), kind=kOutput, calls=%fused_computation.22 | convolution fusion | flops 536870912 | bytes 5242880 | tf_op jit(solution)/shard_map/dot_general | solution.py:173
  16.1 4.3 %collective-permute-done = f32[128,273]{0,1:T(8,128)S(1)} collective-permute-done((f32[128,273]{0,1:T(8,128)S(1)}, f32[128,273]{0,1:T(8,128)S(1)}, u32[]{:S(2)}, u32[]{:S(2)}) %collective-permute-start) | collective-permute-done | bytes 139808 | tf_op jit(solution)/shard_map/ppermute | solution.py:19
  22.2 3.9 %collective-permute-start.6 = (f32[16,64,128]{2,1,0:T(8,128)S(1)}, f32[16,64,128]{2,1,0:T(8,128)}, u32[]{:S(2)}, u32[]{:S(2)}) collective-permute-start(f32[16,64,128]{2,1,0:T(8,128)S(1)} %fusion.76), channel_id=1, source_target_pairs={{0,2},{2,4},{4,6},{6,8},{8,10},{10,12},{12,14},{14,16},{16,18},{18... | collective-permute-start | bytes 1572872 | tf_op jit(solution)/shard_map/ppermute | solution.py:15
  26.2 14.1 %collective-permute-done.6 = f32[16,64,128]{2,1,0:T(8,128)} collective-permute-done((f32[16,64,128]{2,1,0:T(8,128)S(1)}, f32[16,64,128]{2,1,0:T(8,128)}, u32[]{:S(2)}, u32[]{:S(2)}) %collective-permute-start.6) | collective-permute-done | bytes 524320 | tf_op jit(solution)/shard_map/ppermute | solution.py:15
  40.3 1.2 multiply_add_fusion.5
  41.5 1.3 collective-permute-start.7
  42.8 1.9 collective-permute-start.1
  44.7 9.4 %collective-permute-done.1 = f32[16]{0:T(128)S(1)} collective-permute-done((f32[16]{0:T(128)S(1)}, f32[16]{0:T(128)S(1)}, u32[]{:S(2)}, u32[]{:S(2)}) %collective-permute-start.1) | collective-permute-done | bytes 96 | tf_op jit(solution)/shard_map/ppermute | solution.py:15
  56.0 1.2 multiply_add_fusion.4
  57.2 1.3 collective-permute-start.8
  58.5 1.3 collective-permute-start.2
  59.8 3.1 %collective-permute-done.2 = f32[16]{0:T(128)S(1)} collective-permute-done((f32[16]{0:T(128)}, f32[16]{0:T(128)S(1)}, u32[]{:S(2)}, u32[]{:S(2)}) %collective-permute-start.2) | collective-permute-done | bytes 96 | tf_op jit(solution)/shard_map/ppermute | solution.py:15
  63.6 23.5 %collective-permute-done.8 = f32[16,64,128]{2,1,0:T(8,128)S(1)} collective-permute-done((f32[16,64,128]{2,1,0:T(8,128)S(1)}, f32[16,64,128]{2,1,0:T(8,128)S(1)}, u32[]{:S(2)}, u32[]{:S(2)}) %collective-permute-start.8) | collective-permute-done | bytes 524320 | tf_op jit(solution)/shard_map/ppermute | solution.py:15
  87.1 1.3 multiply_add_fusion.3
  88.4 1.3 collective-permute-start.9
  89.8 1.3 collective-permute-start.3
  91.1 6.9 %collective-permute-done.3 = f32[16]{0:T(128)S(1)} collective-permute-done((f32[16]{0:T(128)}, f32[16]{0:T(128)S(1)}, u32[]{:S(2)}, u32[]{:S(2)}) %collective-permute-start.3) | collective-permute-done | bytes 96 | tf_op jit(solution)/shard_map/ppermute | solution.py:15
  98.7 6.3 %collective-permute-done.9 = f32[16,64,128]{2,1,0:T(8,128)} collective-permute-done((f32[16,64,128]{2,1,0:T(8,128)S(1)}, f32[16,64,128]{2,1,0:T(8,128)}, u32[]{:S(2)}, u32[]{:S(2)}) %collective-permute-start.9) | collective-permute-done | bytes 524320 | tf_op jit(solution)/shard_map/ppermute | solution.py:15
  105.0 1.2 multiply_add_fusion.2
  106.2 1.4 collective-permute-start.10
  109.5 1.4 mul.334
  110.9 1.3 constant_dynamic-slice_fusion.12
  112.8 1.3 collective-permute-start.4
  114.1 1.4 mul.308
  115.4 7.6 %collective-permute-done.4 = f32[16]{0:T(128)} collective-permute-done((f32[16]{0:T(128)}, f32[16]{0:T(128)}, u32[]{:S(2)}, u32[]{:S(2)}) %collective-permute-start.4) | collective-permute-done | bytes 96 | tf_op jit(solution)/shard_map/ppermute | solution.py:15
  124.7 1.9 multiply_add_fusion.1
  126.6 1.3 collective-permute-start.11
  130.0 3.0 %fusion.19 = f32[16,64,128]{2,1,0:T(8,128)S(1)} fusion(f32[128,16,64]{0,2,1:T(8,128)S(1)} %bitcast.158, f32[16,128]{1,0:T(8,128)} %get-tuple-element.107, f32[128,128]{1,0:T(8,128)S(1)} %convolution_multiply_fusion, f32[16,128]{1,0:T(8,128)S(1)} %copy.52, pred[128,128]{1,0:T(8,128)(4,1)} %iota_compare_fusion), kind=kOutput, calls=%fused_computation.25 | convolution fusion | flops 202637312 | bytes 1146880 | tf_op jit(solution)/shard_map/gkts,sgkp->tgkp/dot_general | solution.py:40
  133.0 1.3 collective-permute-start.5
  134.4 11.9 %collective-permute-done.5 = f32[16]{0:T(128)S(1)} collective-permute-done((f32[16]{0:T(128)}, f32[16]{0:T(128)S(1)}, u32[]{:S(2)}, u32[]{:S(2)}) %collective-permute-start.5) | collective-permute-done | bytes 96 | tf_op jit(solution)/shard_map/ppermute | solution.py:15
  146.9 1.7 collective-permute-done.11
  148.6 3.4 %fusion.29 = (f32[128,16]{0,1:T(8,128)S(1)}, f32[16,64,128]{2,1,0:T(8,128)}) fusion(f32[16,64,128]{2,1,0:T(8,128)S(1)} %fusion.19, f32[16]{0:T(128)} %copy-done.14, f32[128,16]{0,1:T(8,128)S(1)} %copy.54, f32[128,1024]{0,1:T(8,128)S(1)} %get-tuple-element.98, f32[128,273]{0,1:T(8,128)} %copy-done.6, f32[128]{0:T(128)S(1)} %fusion.88, ...), kind=kOutput, calls=%fused_computation.38 | convolution fusion | flops 204355584 | bytes 4802310 | tf_op jit(solution)/shard_map/tgn,gkpn->tgkp/dot_general | solution.py:63
  152.6 33.1 %all-gather.2.cloned.1.call-done = bf16[8192,4,128]{2,0,1:T(8,128)(2,1)} async-done(((bf16[128,4,128]{2,0,1:T(8,128)(2,1)}), bf16[8192,4,128]{2,0,1:T(8,128)(2,1)}) %all-gather.2.cloned.1.call-update) | async-done | bytes 8388624 | tf_op jit(solution)/shard_map/all_gather | solution.py:106
  185.8 72.2 %while.15 = (s32[]{:T(128)}, f32[2,4,128]{2,1,0:T(4,128)S(1)}, f32[2,4,128]{2,1,0:T(4,128)S(1)}, f32[2,4,128,128]{3,2,1,0:T(8,128)S(1)}, s32[]{:T(128)}, /*index...) while((s32[]{:T(128)}, f32[2,4,128]{2,1,0:T(4,128)S(1)}, ...), condition=%wide.region_6.7_spmd.clone, body=%wide.region_3.6_spmd.clone.sunk | while | flops 550898816 | bytes 32318704 | solution.py:141
  186.3 1.8 fusion.116
  188.1 2.0 copy-done.1
  191.2 3.9 %fusion.118 = f32[2,4,128,128]{3,2,1,0:T(8,128)S(1)} fusion(f32[2,1024,4,128]{3,1,2,0:T(8,128)} %copy-done.1, f32[2,4,128]{2,1,0:T(4,128)S(1)} %max.29, pred[128,1024]{0,1:T(8,128)(4,1)S(1)} %broadcast_compare_fusion.2, bf16[8192,4,128]{2,0,1:T(8,128)(2,1)} %get-tuple-element.210, s32[]{:T(128)S(6)} %select_n.373, s32[]{:T(128)S(6)} %add.345, ...), kind=kOutput, calls=%fused_computation.8.clone.1 | convolution fusion | flops 273940480 | bytes 5906440 | tf_op jit(solution)/shard_map/while/body/kgqs,skd->kgqd/dot_general | solution.py:127
  195.3 1.8 fusion.116
  197.1 2.0 copy-done.1
  200.2 3.9 %fusion.118 = f32[2,4,128,128]{3,2,1,0:T(8,128)S(1)} fusion(f32[2,1024,4,128]{3,1,2,0:T(8,128)} %copy-done.1, f32[2,4,128]{2,1,0:T(4,128)S(1)} %max.29, pred[128,1024]{0,1:T(8,128)(4,1)S(1)} %broadcast_compare_fusion.2, bf16[8192,4,128]{2,0,1:T(8,128)(2,1)} %get-tuple-element.210, s32[]{:T(128)S(6)} %select_n.373, s32[]{:T(128)S(6)} %add.345, ...), kind=kOutput, calls=%fused_computation.8.clone.1 | convolution fusion | flops 273940480 | bytes 5906440 | tf_op jit(solution)/shard_map/while/body/kgqs,skd->kgqd/dot_general | solution.py:127
  204.3 1.8 fusion.116
  206.1 2.0 copy-done.1
  209.2 3.9 %fusion.118 = f32[2,4,128,128]{3,2,1,0:T(8,128)S(1)} fusion(f32[2,1024,4,128]{3,1,2,0:T(8,128)} %copy-done.1, f32[2,4,128]{2,1,0:T(4,128)S(1)} %max.29, pred[128,1024]{0,1:T(8,128)(4,1)S(1)} %broadcast_compare_fusion.2, bf16[8192,4,128]{2,0,1:T(8,128)(2,1)} %get-tuple-element.210, s32[]{:T(128)S(6)} %select_n.373, s32[]{:T(128)S(6)} %add.345, ...), kind=kOutput, calls=%fused_computation.8.clone.1 | convolution fusion | flops 273940480 | bytes 5906440 | tf_op jit(solution)/shard_map/while/body/kgqs,skd->kgqd/dot_general | solution.py:127
  213.3 1.8 fusion.116
  215.1 2.0 copy-done.1
  218.2 3.9 %fusion.118 = f32[2,4,128,128]{3,2,1,0:T(8,128)S(1)} fusion(f32[2,1024,4,128]{3,1,2,0:T(8,128)} %copy-done.1, f32[2,4,128]{2,1,0:T(4,128)S(1)} %max.29, pred[128,1024]{0,1:T(8,128)(4,1)S(1)} %broadcast_compare_fusion.2, bf16[8192,4,128]{2,0,1:T(8,128)(2,1)} %get-tuple-element.210, s32[]{:T(128)S(6)} %select_n.373, s32[]{:T(128)S(6)} %add.345, ...), kind=kOutput, calls=%fused_computation.8.clone.1 | convolution fusion | flops 273940480 | bytes 5906440 | tf_op jit(solution)/shard_map/while/body/kgqs,skd->kgqd/dot_general | solution.py:127
  222.3 1.8 fusion.116
  224.1 2.0 copy-done.1
  227.2 3.9 %fusion.118 = f32[2,4,128,128]{3,2,1,0:T(8,128)S(1)} fusion(f32[2,1024,4,128]{3,1,2,0:T(8,128)} %copy-done.1, f32[2,4,128]{2,1,0:T(4,128)S(1)} %max.29, pred[128,1024]{0,1:T(8,128)(4,1)S(1)} %broadcast_compare_fusion.2, bf16[8192,4,128]{2,0,1:T(8,128)(2,1)} %get-tuple-element.210, s32[]{:T(128)S(6)} %select_n.373, s32[]{:T(128)S(6)} %add.345, ...), kind=kOutput, calls=%fused_computation.8.clone.1 | convolution fusion | flops 273940480 | bytes 5906440 | tf_op jit(solution)/shard_map/while/body/kgqs,skd->kgqd/dot_general | solution.py:127
  231.3 1.8 fusion.116
  233.1 2.0 copy-done.1
  236.2 3.9 %fusion.118 = f32[2,4,128,128]{3,2,1,0:T(8,128)S(1)} fusion(f32[2,1024,4,128]{3,1,2,0:T(8,128)} %copy-done.1, f32[2,4,128]{2,1,0:T(4,128)S(1)} %max.29, pred[128,1024]{0,1:T(8,128)(4,1)S(1)} %broadcast_compare_fusion.2, bf16[8192,4,128]{2,0,1:T(8,128)(2,1)} %get-tuple-element.210, s32[]{:T(128)S(6)} %select_n.373, s32[]{:T(128)S(6)} %add.345, ...), kind=kOutput, calls=%fused_computation.8.clone.1 | convolution fusion | flops 273940480 | bytes 5906440 | tf_op jit(solution)/shard_map/while/body/kgqs,skd->kgqd/dot_general | solution.py:127
  240.3 1.8 fusion.116
  242.2 2.0 copy-done.1
  245.2 3.9 %fusion.118 = f32[2,4,128,128]{3,2,1,0:T(8,128)S(1)} fusion(f32[2,1024,4,128]{3,1,2,0:T(8,128)} %copy-done.1, f32[2,4,128]{2,1,0:T(4,128)S(1)} %max.29, pred[128,1024]{0,1:T(8,128)(4,1)S(1)} %broadcast_compare_fusion.2, bf16[8192,4,128]{2,0,1:T(8,128)(2,1)} %get-tuple-element.210, s32[]{:T(128)S(6)} %select_n.373, s32[]{:T(128)S(6)} %add.345, ...), kind=kOutput, calls=%fused_computation.8.clone.1 | convolution fusion | flops 273940480 | bytes 5906440 | tf_op jit(solution)/shard_map/while/body/kgqs,skd->kgqd/dot_general | solution.py:127
  249.3 1.8 fusion.116
  251.2 2.0 copy-done.1
  254.2 3.9 %fusion.118 = f32[2,4,128,128]{3,2,1,0:T(8,128)S(1)} fusion(f32[2,1024,4,128]{3,1,2,0:T(8,128)} %copy-done.1, f32[2,4,128]{2,1,0:T(4,128)S(1)} %max.29, pred[128,1024]{0,1:T(8,128)(4,1)S(1)} %broadcast_compare_fusion.2, bf16[8192,4,128]{2,0,1:T(8,128)(2,1)} %get-tuple-element.210, s32[]{:T(128)S(6)} %select_n.373, s32[]{:T(128)S(6)} %add.345, ...), kind=kOutput, calls=%fused_computation.8.clone.1 | convolution fusion | flops 273940480 | bytes 5906440 | tf_op jit(solution)/shard_map/while/body/kgqs,skd->kgqd/dot_general | solution.py:127
  260.1 1.4 bitcast_select_fusion.2
  261.5 1.9 collective-permute-start.12
  263.4 1.2 collective-permute-done.12
  (144 shorter events, 27.3 us)
Async XLA Ops:
  6.5 83.2 %copy-start = (bf16[128,16,128]{2,1,0:T(8,128)(2,1)S(1)}, bf16[128,16,128]{2,1,0:T(8,128)(2,1)}, u32[]{:S(2)}) copy-start(bf16[128,16,128]{2,1,0:T(8,128)(2,1)} %param.12) | copy-start | bytes 1572868
  6.5 179.3 %all-gather.2.cloned.1.call-start = ((), (), s32[]{:S(2)}) async-start(), calls=%async_computation | async-start | bytes 8519680 | tf_op jit(solution)/shard_map/all_gather | solution.py:106
  11.2 4.8 %copy-start.15 = (f32[1,32]{1,0:T(1,128)S(1)}, f32[1,32]{1,0:T(1,128)}, u32[]{:S(2)}) copy-start(f32[1,32]{1,0:T(1,128)} %param.18) | copy-start | bytes 388
  11.2 4.8 %copy-start.16 = (f32[1,32]{1,0:T(1,128)S(1)}, f32[1,32]{1,0:T(1,128)}, u32[]{:S(2)}) copy-start(f32[1,32]{1,0:T(1,128)} %param.19) | copy-start | bytes 388
  15.7 4.7 %collective-permute-start = (f32[128,273]{0,1:T(8,128)S(1)}, f32[128,273]{0,1:T(8,128)S(1)}, u32[]{:S(2)}, u32[]{:S(2)}) collective-permute-start(f32[128,273]{0,1:T(8,128)S(1)} %pad_maximum_fusion), channel_id=1, source_target_pairs={{0,1},{1,0},{2,3},{3,2},{4,5},{5,4},{6,7},{7,6},{8,9},{9,8},{10,11... | collective-permute-start | bytes 419336 | tf_op jit(solution)/shard_map/ppermute | solution.py:19
  20.4 107.5 %copy-start.6 = (f32[128,273]{0,1:T(8,128)}, f32[128,273]{0,1:T(8,128)S(1)}, u32[]{:S(2)}) copy-start(f32[128,273]{0,1:T(8,128)S(1)} %fusion.74) | copy-start | bytes 419332
  20.8 35.2 %copy-start.7 = (f32[128,16]{1,0:T(8,128)}, f32[128,16]{1,0:T(8,128)S(1)}, u32[]{:S(2)}) copy-start(f32[128,16]{1,0:T(8,128)S(1)} %reduce_window_sum.11) | copy-start | bytes 24580
  22.2 18.1 %collective-permute-start.6 = (f32[16,64,128]{2,1,0:T(8,128)S(1)}, f32[16,64,128]{2,1,0:T(8,128)}, u32[]{:S(2)}, u32[]{:S(2)}) collective-permute-start(f32[16,64,128]{2,1,0:T(8,128)S(1)} %fusion.76), channel_id=1, source_target_pairs={{0,2},{2,4},{4,6},{6,8},{8,10},{10,12},{12,14},{14,16},{16,18},{18... | collective-permute-start | bytes 1572872 | tf_op jit(solution)/shard_map/ppermute | solution.py:15
  41.5 13.8 %collective-permute-start.7 = (f32[16,64,128]{2,1,0:T(8,128)S(1)}, f32[16,64,128]{2,1,0:T(8,128)S(1)}, u32[]{:S(2)}, u32[]{:S(2)}) collective-permute-start(f32[16,64,128]{2,1,0:T(8,128)S(1)} %multiply_add_fusion.5), channel_id=1, source_target_pairs={{0,4},{2,6},{4,8},{6,10},{8,12},{10,14},{12,16},{14,18},{16,20},{1... | collective-permute-start | bytes 1572872 | tf_op jit(solution)/shard_map/ppermute | solution.py:15
  42.8 11.3 %collective-permute-start.1 = (f32[16]{0:T(128)S(1)}, f32[16]{0:T(128)S(1)}, u32[]{:S(2)}, u32[]{:S(2)}) collective-permute-start(f32[16]{0:T(128)S(1)} %fusion.97), channel_id=1, source_target_pairs={{0,2},{2,4},{4,6},{6,8},{8,10},{10,12},{12,14},{14,16},{16,18},{18... | collective-permute-start | bytes 200 | tf_op jit(solution)/shard_map/ppermute | solution.py:15
  55.2 0.8 copy-start.3
  57.2 6.4 %copy-start.2 = (f32[16,64,128]{2,1,0:T(8,128)}, f32[16,64,128]{2,1,0:T(8,128)S(1)}, u32[]{:S(2)}) copy-start(f32[16,64,128]{2,1,0:T(8,128)S(1)} %multiply_add_fusion.4) | copy-start | bytes 1572868
  57.2 29.8 %collective-permute-start.8 = (f32[16,64,128]{2,1,0:T(8,128)S(1)}, f32[16,64,128]{2,1,0:T(8,128)S(1)}, u32[]{:S(2)}, u32[]{:S(2)}) collective-permute-start(f32[16,64,128]{2,1,0:T(8,128)S(1)} %multiply_add_fusion.4), channel_id=1, source_target_pairs={{0,8},{2,10},{4,12},{6,14},{8,16},{10,18},{12,20},{14,22},{16,24},... | collective-permute-start | bytes 1572872 | tf_op jit(solution)/shard_map/ppermute | solution.py:15
  58.5 4.4 %collective-permute-start.2 = (f32[16]{0:T(128)}, f32[16]{0:T(128)S(1)}, u32[]{:S(2)}, u32[]{:S(2)}) collective-permute-start(f32[16]{0:T(128)} %get-tuple-element.95), channel_id=1, source_target_pairs={{0,4},{2,6},{4,8},{6,10},{8,12},{10,14},{12,16},{14,18},{16,20},{1... | collective-permute-start | bytes 200 | tf_op jit(solution)/shard_map/ppermute | solution.py:15
  62.9 0.6 copy-start.12
  63.6 23.5 %copy-start.9 = (f32[16]{0:T(128)}, f32[16]{0:T(128)S(1)}, u32[]{:S(2)}) copy-start(f32[16]{0:T(128)S(1)} %fusion.94) | copy-start | bytes 196
  87.1 11.6 %copy-start.4 = (f32[16,64,128]{2,1,0:T(8,128)}, f32[16,64,128]{2,1,0:T(8,128)S(1)}, u32[]{:S(2)}) copy-start(f32[16,64,128]{2,1,0:T(8,128)S(1)} %collective-permute-done.8) | copy-start | bytes 1572868
  88.4 16.6 %collective-permute-start.9 = (f32[16,64,128]{2,1,0:T(8,128)S(1)}, f32[16,64,128]{2,1,0:T(8,128)}, u32[]{:S(2)}, u32[]{:S(2)}) collective-permute-start(f32[16,64,128]{2,1,0:T(8,128)S(1)} %multiply_add_fusion.3), channel_id=1, source_target_pairs={{0,16},{2,18},{4,20},{6,22},{8,24},{10,26},{12,28},{14,30},{16,32}... | collective-permute-start | bytes 1572872 | tf_op jit(solution)/shard_map/ppermute | solution.py:15
  89.8 8.3 %collective-permute-start.3 = (f32[16]{0:T(128)}, f32[16]{0:T(128)S(1)}, u32[]{:S(2)}, u32[]{:S(2)}) collective-permute-start(f32[16]{0:T(128)} %copy-done.9), channel_id=1, source_target_pairs={{0,8},{2,10},{4,12},{6,14},{8,16},{10,18},{12,20},{14,22},{16,24},... | collective-permute-start | bytes 200 | tf_op jit(solution)/shard_map/ppermute | solution.py:15
  98.0 0.6 copy-start.13
  98.7 7.5 %copy-start.10 = (f32[16]{0:T(128)}, f32[16]{0:T(128)S(1)}, u32[]{:S(2)}) copy-start(f32[16]{0:T(128)S(1)} %fusion.92) | copy-start | bytes 196
  106.2 42.4 %copy-start.5 = (f32[16,64,128]{2,1,0:T(8,128)S(1)}, f32[16,64,128]{2,1,0:T(8,128)}, u32[]{:S(2)}) copy-start(f32[16,64,128]{2,1,0:T(8,128)} %copy-done.4) | copy-start | bytes 1572868
  106.2 18.5 %collective-permute-start.10 = (f32[16,64,128]{2,1,0:T(8,128)S(1)}, f32[16,64,128]{2,1,0:T(8,128)}, u32[]{:S(2)}, u32[]{:S(2)}) collective-permute-start(f32[16,64,128]{2,1,0:T(8,128)S(1)} %multiply_add_fusion.2), channel_id=1, source_target_pairs={{0,32},{2,34},{4,36},{6,38},{8,40},{10,42},{12,44},{14,46},{16,48}... | collective-permute-start | bytes 1572872 | tf_op jit(solution)/shard_map/ppermute | solution.py:15
  108.4 0.5 copy-start.14
  112.8 10.3 %collective-permute-start.4 = (f32[16]{0:T(128)}, f32[16]{0:T(128)}, u32[]{:S(2)}, u32[]{:S(2)}) collective-permute-start(f32[16]{0:T(128)} %copy-done.10), channel_id=1, source_target_pairs={{0,16},{2,18},{4,20},{6,22},{8,24},{10,26},{12,28},{14,30},{16,32}... | collective-permute-start | bytes 200 | tf_op jit(solution)/shard_map/ppermute | solution.py:15
  123.7 5.4 %copy-start.11 = (f32[16]{0:T(128)}, f32[16]{0:T(128)S(1)}, u32[]{:S(2)}) copy-start(f32[16]{0:T(128)S(1)} %fusion.90) | copy-start | bytes 196
  126.6 22.0 %collective-permute-start.11 = (f32[16,64,128]{2,1,0:T(8,128)}, f32[16,64,128]{2,1,0:T(8,128)}, u32[]{:S(2)}, u32[]{:S(2)}) collective-permute-start(f32[16,64,128]{2,1,0:T(8,128)} %multiply_add_fusion.1), channel_id=1, source_target_pairs={{0,64},{2,66},{4,68},{6,70},{8,72},{10,74},{12,76},{14,78},{16,80}... | collective-permute-start | bytes 1572872 | tf_op jit(solution)/shard_map/ppermute | solution.py:15
  133.0 13.3 %collective-permute-start.5 = (f32[16]{0:T(128)}, f32[16]{0:T(128)S(1)}, u32[]{:S(2)}, u32[]{:S(2)}) collective-permute-start(f32[16]{0:T(128)} %copy-done.11), channel_id=1, source_target_pairs={{0,32},{2,34},{4,36},{6,38},{8,40},{10,42},{12,44},{14,46},{16,48}... | collective-permute-start | bytes 200 | tf_op jit(solution)/shard_map/ppermute | solution.py:15
  134.3 51.5 %copy-start.8 = (f32[128,16]{0,1:T(8,128)}, f32[128,16]{0,1:T(8,128)S(1)}, u32[]{:S(2)}) copy-start(f32[128,16]{0,1:T(8,128)S(1)} %copy.54) | copy-start | bytes 24580
  188.1 2.0 copy-start.1
  197.1 2.0 copy-start.1
  206.1 2.0 copy-start.1
  215.1 2.0 copy-start.1
  224.1 2.0 copy-start.1
  233.1 2.0 copy-start.1
  242.1 2.0 copy-start.1
  251.1 2.0 copy-start.1
  261.5 3.1 %collective-permute-start.12 = (bf16[128,1024]{0,1:T(8,128)(2,1)S(1)}, bf16[128,1024]{0,1:T(8,128)(2,1)S(1)}, u32[]{:S(2)}, u32[]{:S(2)}) collective-permute-start(bf16[128,1024]{0,1:T(8,128)(2,1)S(1)} %get-tuple-element.89), channel_id=1, source_target_pairs={{0,128},{128,0},{1,129},{129,1},{2,130},{130,2},{3,131},{131,3},{4... | collective-permute-start | bytes 786440 | tf_op jit(solution)/shard_map/ppermute | solution.py:19
Sparse Core Ops, SparseCore 0:
  10.9 174.8 all-gather.1
where the time goes:
time: 274 us; the launch traced here: 273 us
  waiting for transfers between devices  125 us (46%)
  matrix products  58.2 us (21%)
  local copies, waits for them, and re-layouts  29.5 us (11%)
  other arithmetic  25.5 us (9%)
  starting transfers between devices  19.8 us (7%)
  between operations  13.8 us (5%)
    ppermute x11, waiting for transfers between devices, shifted_up(): return lax.ppermute(value, axis, pairs)  86.3 us
    all_gather x1, waiting for transfers between devices, attention_half(): both_all = lax.all_gather(both, 'ctx', axis=0, tiled=True)  33.1 us
    dot_general x8, matrix products, add_block(): jnp.einsum('kgqs,skd->kgqd', raw_weight.astype(jnp.bfloat16), value_block...  30.9 us
    ppermute x11, starting transfers between devices, shifted_up(): return lax.ppermute(value, axis, pairs)  17.6 us
    while x24, local copies, waits for them, and re-layouts  15.9 us
    dot_general x8, matrix products, add_block(): jnp.einsum('kgqd,skd->kgqs', grouped, key_block, preferred_element_type=j...  14.5 us
    reduce_sum x8, other arithmetic, add_block(): new_total = row_total * factor + jnp.sum(raw_weight, axis=3)  8.18 us
    add x5, other arithmetic, merge_states(): later[0][:, None, None] * earlier[1] + later[1]  6.77 us
  transfers between devices with their start and end apart: 14, of which 14 were waited for; matrix products, arithmetic and copies ran while one was open for 13% of the time, Pallas kernels for 0%

commit v1 on v0

--- a/solution.py
+++ b/solution.py
@@ -103,7 +103,9 @@
     query_place = first_row + jnp.arange(row_count, dtype=jnp.int32)
     grouped = queries.reshape(row_count, kv_heads, group_size, head_width).transpose(1, 2, 0, 3)
     both = jnp.concatenate([keys, values], axis=1)
-    both_all = lax.all_gather(both, "ctx", axis=0, tiled=True)
+    both_all = jnp.concatenate(
+        lax.all_to_all(jnp.stack([both] * lax.axis_size("ctx")), "ctx", 0, 0), axis=0
+    )
     key_count = both_all.shape[0]
     block_size = math.gcd(key_count, 1024)
 

time: 274 us -> 420 us (1.53)
  waiting for transfers between devices: 125 us -> 272 us
  between operations: 13.8 us -> 0.46 us
  starting transfers between devices: 19.8 us -> 32.6 us
  local copies, waits for them, and re-layouts: 29.5 us -> 35.4 us
  other arithmetic: 25.5 us -> 20.5 us
    ppermute x11, waiting for transfers between devices: 86.3 us -> 253 us  [shifted_up(): return lax.ppermute(value, axis, pairs)]
    all_gather x1 -> x0, waiting for transfers between devices: 33.1 us -> none  [attention_half(): both_all = lax.all_gather(both, 'ctx', axis=0, tiled=True)]
    ppermute x2, waiting for transfers between devices: 5.47 us -> 18.9 us  [swapped(): return lax.ppermute(value, axis, [(0, 1), (1, 0)])]
    all_to_all x0 -> x1, starting transfers between devices: none -> 10.6 us  [attention_half(): lax.all_to_all(jnp.stack([both] * lax.axis_size('ctx')), 'ctx', 0, 0)]
    all_to_all x0 -> x1, local copies, waits for them, and re-layouts: none -> 10.3 us  [attention_half(): lax.all_to_all(jnp.stack([both] * lax.axis_size('ctx')), 'ctx', 0, 0)]
    another operation x0 -> x1, local copies, waits for them, and re-layouts: none -> 5.35 us  [attention_half(): jnp.stack([both] * lax.axis_size('ctx'))]
  transfers between devices with their start and end apart: 14 -> 14, of which waited for: 14 -> 13; matrix products, arithmetic and copies ran while one was open for 13% -> 5% of each run, Pallas kernels for 0% -> 0%
where the time goes in v1:
time: 420 us; the launch traced here: 418 us
  waiting for transfers between devices  272 us (65%)
  matrix products  56.3 us (13%)
  local copies, waits for them, and re-layouts  35.4 us (8%)
  starting transfers between devices  32.6 us (8%)
  other arithmetic  20.5 us (5%)
    ppermute x11, waiting for transfers between devices, shifted_up(): return lax.ppermute(value, axis, pairs)  253 us
    dot_general x8, matrix products, add_block(): jnp.einsum('kgqs,skd->kgqd', raw_weight.astype(jnp.bfloat16), value_block...  30.9 us
    ppermute x2, waiting for transfers between devices, swapped(): return lax.ppermute(value, axis, [(0, 1), (1, 0)])  18.9 us
    ppermute x11, starting transfers between devices, shifted_up(): return lax.ppermute(value, axis, pairs)  18.7 us
    while x24, local copies, waits for them, and re-layouts  15.4 us
    dot_general x8, matrix products, add_block(): jnp.einsum('kgqd,skd->kgqs', grouped, key_block, preferred_element_type=j...  14.6 us
    all_to_all x1, starting transfers between devices, attention_half(): lax.all_to_all(jnp.stack([both] * lax.axis_size('ctx')), 'ctx', 0, 0)  10.6 us
    all_to_all x1, local copies, waits for them, and re-layouts, attention_half(): lax.all_to_all(jnp.stack([both] * lax.axis_size('ctx')), 'ctx', 0, 0)  10.3 us
  transfers between devices with their start and end apart: 14, of which 13 were waited for; matrix products, arithmetic and copies ran while one was open for 5% of the time, Pallas kernels for 0%

profile of v1, /device:TPU:239, one launch (start us, length us, event | category | flops | bytes accessed | tf_op | source)
XLA Modules:
  0.0 418.3 jit_solution(1201703176398546880)
XLA Ops:
  0.0 1.2 constant_dynamic-slice_fusion.1
  1.3 5.3 %stack.2 = bf16[64,128,4,128]{3,1,2,0:T(8,128)(2,1)} broadcast(bf16[128,4,128]{2,0,1:T(8,128)(2,1)S(1)} %copy.87), dimensions={1,2,3} | broadcast | bytes 8519680 | tf_op jit(solution)/shard_map/stack | solution.py:107
  6.7 10.6 %all-to-all-start = ((bf16[64,128,4,128]{3,1,2,0:T(8,128)(2,1)}), bf16[64,128,4,128]{3,1,2,0:T(8,128)(2,1)}, u32[]{:S(2)}, u32[]{:S(2)}) async-start(bf16[64,128,4,128]{3,1,2,0:T(8,128)(2,1)} %stack.2), calls=%async_computation | async-start | bytes 16777216 | tf_op jit(solution)/shard_map/all_to_all | solution.py:107
  17.9 3.9 fusion.17
  22.2 1.2 collective-permute-start
  23.5 17.7 %collective-permute-done = f32[128,273]{0,1:T(8,128)S(1)} collective-permute-done((f32[128,273]{0,1:T(8,128)S(1)}, f32[128,273]{0,1:T(8,128)S(1)}, u32[]{:S(2)}, u32[]{:S(2)}) %collective-permute-start) | collective-permute-done | bytes 139808 | tf_op jit(solution)/shard_map/ppermute | solution.py:19
  42.5 5.0 %collective-permute-start.6 = (f32[16,64,128]{2,1,0:T(8,128)S(1)}, f32[16,64,128]{2,1,0:T(8,128)}, u32[]{:S(2)}, u32[]{:S(2)}) collective-permute-start(f32[16,64,128]{2,1,0:T(8,128)S(1)} %fusion.76), channel_id=1, source_target_pairs={{0,2},{2,4},{4,6},{6,8},{8,10},{10,12},{12,14},{14,16},{16,18},{18... | collective-permute-start | bytes 1572872 | tf_op jit(solution)/shard_map/ppermute | solution.py:15
  47.6 165.3 %collective-permute-done.6 = f32[16,64,128]{2,1,0:T(8,128)} collective-permute-done((f32[16,64,128]{2,1,0:T(8,128)S(1)}, f32[16,64,128]{2,1,0:T(8,128)}, u32[]{:S(2)}, u32[]{:S(2)}) %collective-permute-start.6) | collective-permute-done | bytes 524320 | tf_op jit(solution)/shard_map/ppermute | solution.py:15
  212.9 1.2 multiply_add_fusion.5
  214.0 1.3 collective-permute-start.7
  215.3 1.9 collective-permute-start.1
  217.3 8.5 %collective-permute-done.1 = f32[16]{0:T(128)S(1)} collective-permute-done((f32[16]{0:T(128)S(1)}, f32[16]{0:T(128)S(1)}, u32[]{:S(2)}, u32[]{:S(2)}) %collective-permute-start.1) | collective-permute-done | bytes 96 | tf_op jit(solution)/shard_map/ppermute | solution.py:15
  225.7 2.2 collective-permute-done.7
  228.8 1.2 multiply_add_fusion.4
  229.9 1.3 collective-permute-start.8
  231.2 1.3 collective-permute-start.2
  232.5 3.0 collective-permute-done.2
  235.6 22.0 %collective-permute-done.8 = f32[16,64,128]{2,1,0:T(8,128)} collective-permute-done((f32[16,64,128]{2,1,0:T(8,128)S(1)}, f32[16,64,128]{2,1,0:T(8,128)}, u32[]{:S(2)}, u32[]{:S(2)}) %collective-permute-start.8) | collective-permute-done | bytes 524320 | tf_op jit(solution)/shard_map/ppermute | solution.py:15
  257.5 1.2 multiply_add_fusion.3
  258.7 1.3 collective-permute-start.9
  260.0 1.3 collective-permute-start.3
  261.4 4.4 %collective-permute-done.3 = f32[16]{0:T(128)S(1)} collective-permute-done((f32[16]{0:T(128)S(1)}, f32[16]{0:T(128)S(1)}, u32[]{:S(2)}, u32[]{:S(2)}) %collective-permute-start.3) | collective-permute-done | bytes 96 | tf_op jit(solution)/shard_map/ppermute | solution.py:15
  265.8 10.3 %collective-permute-done.9 = f32[16,64,128]{2,1,0:T(8,128)} collective-permute-done((f32[16,64,128]{2,1,0:T(8,128)S(1)}, f32[16,64,128]{2,1,0:T(8,128)}, u32[]{:S(2)}, u32[]{:S(2)}) %collective-permute-start.9) | collective-permute-done | bytes 524320 | tf_op jit(solution)/shard_map/ppermute | solution.py:15
  276.0 2.0 multiply_add_fusion.2
  278.0 1.3 collective-permute-start.10
  279.6 1.3 collective-permute-start.4
  280.9 14.9 %collective-permute-done.4 = f32[16]{0:T(128)S(1)} collective-permute-done((f32[16]{0:T(128)S(1)}, f32[16]{0:T(128)S(1)}, u32[]{:S(2)}, u32[]{:S(2)}) %collective-permute-start.4) | collective-permute-done | bytes 96 | tf_op jit(solution)/shard_map/ppermute | solution.py:15
  295.8 12.4 %collective-permute-done.10 = f32[16,64,128]{2,1,0:T(8,128)S(1)} collective-permute-done((f32[16,64,128]{2,1,0:T(8,128)}, f32[16,64,128]{2,1,0:T(8,128)S(1)}, u32[]{:S(2)}, u32[]{:S(2)}) %collective-permute-start.10) | collective-permute-done | bytes 524320 | tf_op jit(solution)/shard_map/ppermute | solution.py:15
  308.3 2.1 multiply_add_fusion.1
  310.4 1.3 collective-permute-start.11
  312.1 2.2 fusion.19
  314.3 1.5 collective-permute-start.5
  315.9 3.2 collective-permute-done.5
  319.1 7.4 %collective-permute-done.11 = f32[16,64,128]{2,1,0:T(8,128)} collective-permute-done((f32[16,64,128]{2,1,0:T(8,128)}, f32[16,64,128]{2,1,0:T(8,128)}, u32[]{:S(2)}, u32[]{:S(2)}) %collective-permute-start.11) | collective-permute-done | bytes 524320 | tf_op jit(solution)/shard_map/ppermute | solution.py:15
  326.4 3.5 fusion.29
  329.9 10.3 %copy.88 = bf16[64,128,4,128]{3,1,0,2:T(8,128)(2,1)} copy(bf16[64,128,4,128]{3,1,2,0:T(8,128)(2,1)} %all-to-all-done) | data formatting | bytes 16777216 | tf_op jit(solution)/shard_map/all_to_all | solution.py:107
  340.3 71.5 %while.15 = (s32[]{:T(128)}, f32[2,4,128]{2,1,0:T(4,128)S(1)}, f32[2,4,128]{2,1,0:T(4,128)S(1)}, f32[2,4,128,128]{3,2,1,0:T(8,128)S(1)}, s32[]{:T(128)}, /*index...) while((s32[]{:T(128)}, f32[2,4,128]{2,1,0:T(4,128)S(1)}, ...), condition=%wide.region_6.7_spmd.clone, body=%wide.region_3.6_spmd.clone.sunk | while | flops 550898816 | bytes 32318704 | solution.py:143
  340.6 1.8 fusion.116
  342.4 1.9 copy-done.1
  345.4 3.9 fusion.118
  349.5 1.8 fusion.116
  351.4 1.9 copy-done.1
  354.3 3.9 fusion.118
  358.5 1.8 fusion.116
  360.3 1.9 copy-done.1
  363.3 3.9 fusion.118
  367.4 1.8 fusion.116
  369.2 1.9 copy-done.1
  372.2 3.9 fusion.118
  376.3 1.8 fusion.116
  378.2 1.9 copy-done.1
  381.2 3.9 fusion.118
  385.3 1.8 fusion.116
  387.1 1.9 copy-done.1
  390.1 3.9 fusion.118
  394.2 1.8 fusion.116
  396.1 1.9 copy-done.1
  399.0 3.9 fusion.118
  403.2 1.8 fusion.116
  405.0 1.9 copy-done.1
  408.0 3.9 fusion.118
  412.3 1.6 bitcast_select_fusion.2
  413.8 2.1 collective-permute-start.12
  416.0 1.2 collective-permute-done.12
  (132 shorter events, 15.7 us)
Async XLA Ops:
  0.0 260.0 %copy-start = (bf16[128,16,128]{2,1,0:T(8,128)(2,1)S(1)}, bf16[128,16,128]{2,1,0:T(8,128)(2,1)}, u32[]{:S(2)}) copy-start(bf16[128,16,128]{2,1,0:T(8,128)(2,1)} %param.12) | copy-start | bytes 1572868
  6.7 10.6 %copy-start.2 = (bf16[128,2048]{1,0:T(8,128)(2,1)S(1)}, bf16[128,2048]{1,0:T(8,128)(2,1)}, u32[]{:S(2)}) copy-start(bf16[128,2048]{1,0:T(8,128)(2,1)} %param.15) | copy-start | bytes 1572868
  6.7 10.9 %copy-start.6 = (bf16[1,2048,64]{1,2,0:T(8,128)(2,1)S(1)}, bf16[1,2048,64]{1,2,0:T(8,128)(2,1)}, u32[]{:S(2)}) copy-start(bf16[1,2048,64]{1,2,0:T(8,128)(2,1)} %param.17) | copy-start | bytes 786436
  6.7 323.2 %all-to-all-start = ((bf16[64,128,4,128]{3,1,2,0:T(8,128)(2,1)}), bf16[64,128,4,128]{3,1,2,0:T(8,128)(2,1)}, u32[]{:S(2)}, u32[]{:S(2)}) async-start(bf16[64,128,4,128]{3,1,2,0:T(8,128)(2,1)} %stack.2), calls=%async_computation | async-start | bytes 16777216 | tf_op jit(solution)/shard_map/all_to_all | solution.py:107
  17.9 5.6 %copy-start.8 = (f32[1,32]{1,0:T(1,128)S(1)}, f32[1,32]{1,0:T(1,128)}, u32[]{:S(2)}) copy-start(f32[1,32]{1,0:T(1,128)} %param.18) | copy-start | bytes 388
  17.9 5.5 %copy-start.9 = (f32[1,32]{1,0:T(1,128)S(1)}, f32[1,32]{1,0:T(1,128)}, u32[]{:S(2)}) copy-start(f32[1,32]{1,0:T(1,128)} %param.19) | copy-start | bytes 388
  22.2 19.0 %collective-permute-start = (f32[128,273]{0,1:T(8,128)S(1)}, f32[128,273]{0,1:T(8,128)S(1)}, u32[]{:S(2)}, u32[]{:S(2)}) collective-permute-start(f32[128,273]{0,1:T(8,128)S(1)} %pad_maximum_fusion), channel_id=1, source_target_pairs={{0,1},{1,0},{2,3},{3,2},{4,5},{5,4},{6,7},{7,6},{8,9},{9,8},{10,11... | collective-permute-start | bytes 419336 | tf_op jit(solution)/shard_map/ppermute | solution.py:19
  41.9 237.4 %copy-start.10 = (f32[1,32]{1,0:T(1,128)S(1)}, f32[1,32]{1,0:T(1,128)}, u32[]{:S(2)}) copy-start(f32[1,32]{1,0:T(1,128)} %param.20) | copy-start | bytes 388
  41.9 237.6 %copy-start.7 = (f32[1,32,64]{2,1,0:T(8,128)S(1)}, f32[1,32,64]{2,1,0:T(8,128)}, u32[]{:S(2)}) copy-start(f32[1,32,64]{2,1,0:T(8,128)} %param.21) | copy-start | bytes 24580
  42.5 170.3 %collective-permute-start.6 = (f32[16,64,128]{2,1,0:T(8,128)S(1)}, f32[16,64,128]{2,1,0:T(8,128)}, u32[]{:S(2)}, u32[]{:S(2)}) collective-permute-start(f32[16,64,128]{2,1,0:T(8,128)S(1)} %fusion.76), channel_id=1, source_target_pairs={{0,2},{2,4},{4,6},{6,8},{8,10},{10,12},{12,14},{14,16},{16,18},{18... | collective-permute-start | bytes 1572872 | tf_op jit(solution)/shard_map/ppermute | solution.py:15
  214.0 13.9 %collective-permute-start.7 = (f32[16,64,128]{2,1,0:T(8,128)S(1)}, f32[16,64,128]{2,1,0:T(8,128)S(1)}, u32[]{:S(2)}, u32[]{:S(2)}) collective-permute-start(f32[16,64,128]{2,1,0:T(8,128)S(1)} %multiply_add_fusion.5), channel_id=1, source_target_pairs={{0,4},{2,6},{4,8},{6,10},{8,12},{10,14},{12,16},{14,18},{16,20},{1... | collective-permute-start | bytes 1572872 | tf_op jit(solution)/shard_map/ppermute | solution.py:15
  215.3 10.4 %collective-permute-start.1 = (f32[16]{0:T(128)S(1)}, f32[16]{0:T(128)S(1)}, u32[]{:S(2)}, u32[]{:S(2)}) collective-permute-start(f32[16]{0:T(128)S(1)} %fusion.97), channel_id=1, source_target_pairs={{0,2},{2,4},{4,6},{6,8},{8,10},{10,12},{12,14},{14,16},{16,18},{18... | collective-permute-start | bytes 200 | tf_op jit(solution)/shard_map/ppermute | solution.py:15
  228.0 0.8 copy-start.3
  229.9 27.6 %collective-permute-start.8 = (f32[16,64,128]{2,1,0:T(8,128)S(1)}, f32[16,64,128]{2,1,0:T(8,128)}, u32[]{:S(2)}, u32[]{:S(2)}) collective-permute-start(f32[16,64,128]{2,1,0:T(8,128)S(1)} %multiply_add_fusion.4), channel_id=1, source_target_pairs={{0,8},{2,10},{4,12},{6,14},{8,16},{10,18},{12,20},{14,22},{16,24},... | collective-permute-start | bytes 1572872 | tf_op jit(solution)/shard_map/ppermute | solution.py:15
  231.2 4.3 %collective-permute-start.2 = (f32[16]{0:T(128)S(1)}, f32[16]{0:T(128)S(1)}, u32[]{:S(2)}, u32[]{:S(2)}) collective-permute-start(f32[16]{0:T(128)S(1)} %get-tuple-element.95), channel_id=1, source_target_pairs={{0,4},{2,6},{4,8},{6,10},{8,12},{10,14},{12,16},{14,18},{16,20},{1... | collective-permute-start | bytes 200 | tf_op jit(solution)/shard_map/ppermute | solution.py:15
  258.7 17.4 %collective-permute-start.9 = (f32[16,64,128]{2,1,0:T(8,128)S(1)}, f32[16,64,128]{2,1,0:T(8,128)}, u32[]{:S(2)}, u32[]{:S(2)}) collective-permute-start(f32[16,64,128]{2,1,0:T(8,128)S(1)} %multiply_add_fusion.3), channel_id=1, source_target_pairs={{0,16},{2,18},{4,20},{6,22},{8,24},{10,26},{12,28},{14,30},{16,32}... | collective-permute-start | bytes 1572872 | tf_op jit(solution)/shard_map/ppermute | solution.py:15
  260.0 5.7 %collective-permute-start.3 = (f32[16]{0:T(128)S(1)}, f32[16]{0:T(128)S(1)}, u32[]{:S(2)}, u32[]{:S(2)}) collective-permute-start(f32[16]{0:T(128)S(1)} %fusion.94), channel_id=1, source_target_pairs={{0,8},{2,10},{4,12},{6,14},{8,16},{10,18},{12,20},{14,22},{16,24},... | collective-permute-start | bytes 200 | tf_op jit(solution)/shard_map/ppermute | solution.py:15
  278.0 30.3 %collective-permute-start.10 = (f32[16,64,128]{2,1,0:T(8,128)}, f32[16,64,128]{2,1,0:T(8,128)S(1)}, u32[]{:S(2)}, u32[]{:S(2)}) collective-permute-start(f32[16,64,128]{2,1,0:T(8,128)} %multiply_add_fusion.2), channel_id=1, source_target_pairs={{0,32},{2,34},{4,36},{6,38},{8,40},{10,42},{12,44},{14,46},{16,48}... | collective-permute-start | bytes 1572872 | tf_op jit(solution)/shard_map/ppermute | solution.py:15
  279.6 16.3 %collective-permute-start.4 = (f32[16]{0:T(128)S(1)}, f32[16]{0:T(128)S(1)}, u32[]{:S(2)}, u32[]{:S(2)}) collective-permute-start(f32[16]{0:T(128)S(1)} %fusion.92), channel_id=1, source_target_pairs={{0,16},{2,18},{4,20},{6,22},{8,24},{10,26},{12,28},{14,30},{16,32}... | collective-permute-start | bytes 200 | tf_op jit(solution)/shard_map/ppermute | solution.py:15
  308.3 3.8 copy-start.5
  310.4 16.0 %collective-permute-start.11 = (f32[16,64,128]{2,1,0:T(8,128)}, f32[16,64,128]{2,1,0:T(8,128)}, u32[]{:S(2)}, u32[]{:S(2)}) collective-permute-start(f32[16,64,128]{2,1,0:T(8,128)} %multiply_add_fusion.1), channel_id=1, source_target_pairs={{0,64},{2,66},{4,68},{6,70},{8,72},{10,74},{12,76},{14,78},{16,80}... | collective-permute-start | bytes 1572872 | tf_op jit(solution)/shard_map/ppermute | solution.py:15
  314.3 25.9 %copy-start.4 = (f32[16,64,128]{2,1,0:T(8,128)}, f32[16,64,128]{2,1,0:T(8,128)S(1)}, u32[]{:S(2)}) copy-start(f32[16,64,128]{2,1,0:T(8,128)S(1)} %fusion.19) | copy-start | bytes 1572868
  314.3 4.7 %collective-permute-start.5 = (f32[16]{0:T(128)S(1)}, f32[16]{0:T(128)S(1)}, u32[]{:S(2)}, u32[]{:S(2)}) collective-permute-start(f32[16]{0:T(128)S(1)} %fusion.90), channel_id=1, source_target_pairs={{0,32},{2,34},{4,36},{6,38},{8,40},{10,42},{12,44},{14,46},{16,48}... | collective-permute-start | bytes 200 | tf_op jit(solution)/shard_map/ppermute | solution.py:15
  342.4 1.9 copy-start.1
  351.3 1.9 copy-start.1
  360.3 1.9 copy-start.1
  369.2 1.9 copy-start.1
  378.2 1.9 copy-start.1
  387.1 1.9 copy-start.1
  396.0 1.9 copy-start.1
  405.0 1.9 copy-start.1
  413.8 3.3 collective-permute-start.12
